TPU v7x, 256 devices: a whole 4x4x8 slice. The times are simulated.
256 devices in a mesh: tm: 16 (over z, core), head: 16 (over y, x).
Axes of the slice: x: 4, y: 4, z: 8, core: 2. Of those that a mesh axis runs over, the one named last changes fastest.
Arguments:
- frames: bfloat16 [8192, 2048], P(('tm', 'head')), may hold values from -6 to 6
- log_decay: float32 [8192, 16], P('tm', 'head'), may hold values from -2 to 0, as said below
- w_query: bfloat16 [2048, 2048], P('tm', 'head'), may hold values from -0.125 to 0.125
- w_key: bfloat16 [2048, 2048], P('tm', 'head'), may hold values from -0.125 to 0.125
- w_value: bfloat16 [2048, 2048], P('tm', 'head'), may hold values from -0.125 to 0.125
- w_gate: bfloat16 [2048, 2048], P('tm', 'head'), may hold values from -0.125 to 0.125
- w_out: bfloat16 [2048, 2048], P('head', 'tm'), may hold values from -0.125 to 0.125
Outputs:
- mixed: bfloat16 [8192, 2048], P(('tm', 'head'))
Inputs may be any that keep to these rules, and one draw needn't show every extreme that they name: `log_decay`: strictly negative.
All inputs are finite; a program needn't handle non-finite values.
Results may differ from a plain program's by a relative error of at most 0.015.
Values may be sent and summed in bfloat16 or wider, within the bound.
No kernel may reach another device: no remote copies, remote signals or barrier semaphores. Data moves between devices by JAX's collectives and lax.ppermute only.
A program may use at most 64 MiB of HBM per device.

v0:
```python
import jax
import jax.numpy as jnp
from jax import lax
from jax.sharding import PartitionSpec as P

HEAD_DIM = 128
BLOCK = 512
PAD_ROWS = 8


def prior_state(local_final, log_total, axis):
    heads_here = local_final.shape[0]
    extra = jnp.broadcast_to(log_total[:, None, None], (heads_here, PAD_ROWS, HEAD_DIM))
    packed = jnp.concatenate([local_final, extra], axis=1)
    gathered = lax.all_gather(packed, axis)
    finals = gathered[:, :, :HEAD_DIM, :]
    totals = gathered[:, :, HEAD_DIM, 0]
    count = gathered.shape[0]
    mine = lax.axis_index(axis)
    order = jnp.arange(count, dtype=jnp.int32)
    between = (order[:, None] < order[None, :]) & (order[None, :] < mine)
    exponent = jnp.sum(jnp.where(between[:, :, None], totals[None, :, :], 0.0), axis=1)
    weight = jnp.where((order < mine)[:, None], jnp.exp(exponent), 0.0)
    return jnp.sum(weight[:, :, None, None] * finals, axis=0)


def shards(frames, log_decay, w_query, w_key, w_value, w_gate, w_out):
    head_width = w_query.shape[1]
    joined = lax.all_gather(
        jnp.concatenate([w_query, w_key, w_value, w_gate], axis=1), "tm", axis=0, tiled=True
    )
    projected = jnp.dot(
        lax.all_gather(frames, "head", axis=0, tiled=True),
        joined,
        preferred_element_type=jnp.float32,
    )
    local_len = projected.shape[0]
    heads_here = head_width // HEAD_DIM
    block_count = local_len // BLOCK
    query_blocks = (
        projected[:, :head_width]
        .astype(jnp.bfloat16)
        .reshape(block_count, BLOCK, heads_here, HEAD_DIM)
    )
    key_blocks = (
        projected[:, head_width : 2 * head_width]
        .astype(jnp.bfloat16)
        .reshape(block_count, BLOCK, heads_here, HEAD_DIM)
    )
    value_blocks = (
        projected[:, 2 * head_width : 3 * head_width]
        .astype(jnp.bfloat16)
        .reshape(block_count, BLOCK, heads_here, HEAD_DIM)
    )
    gate_all = projected[:, 3 * head_width :]
    running_blocks = jnp.cumsum(log_decay.reshape(block_count, BLOCK, heads_here), axis=1)
    slice_ordinal = jnp.arange(BLOCK, dtype=jnp.int32)
    causal = slice_ordinal[:, None] >= slice_ordinal[None, :]

    def local_step(carry_state, inputs):
        query_block, key_block, value_block, running = inputs
        gaps = running.T[:, :, None] - running.T[:, None, :]
        decay = jnp.exp(jnp.where(causal[None], gaps, -jnp.inf))
        scores = jnp.einsum(
            "thd,shd->hts", query_block, key_block, preferred_element_type=jnp.float32
        )
        weights = (scores * decay).astype(jnp.bfloat16)
        intra = jnp.einsum("hts,shd->thd", weights, value_block, preferred_element_type=jnp.float32)
        scaled = (
            key_block.astype(jnp.float32) * jnp.exp(running[-1][None, :] - running)[:, :, None]
        ).astype(jnp.bfloat16)
        update = jnp.einsum("shd,she->hde", scaled, value_block, preferred_element_type=jnp.float32)
        next_state = jnp.exp(running[-1])[:, None, None] * carry_state + update
        return (next_state, (intra, carry_state))

    zero_state = jnp.zeros((heads_here, HEAD_DIM, HEAD_DIM), jnp.float32)
    local_final, (intra_all, local_starts) = lax.scan(
        local_step, zero_state, (query_blocks, key_blocks, value_blocks, running_blocks)
    )
    prior = prior_state(local_final, jnp.sum(log_decay, axis=0), "tm")
    block_logs = running_blocks[:, -1, :]
    before = jnp.cumsum(block_logs, axis=0) - block_logs
    start_states = jnp.exp(before)[:, :, None, None] * prior[None] + local_starts
    lifted = query_blocks.astype(jnp.float32) * jnp.exp(running_blocks)[..., None]
    inter = jnp.einsum("cthd,chde->cthe", lifted, start_states, precision=lax.Precision.HIGHEST)
    retained = (intra_all + inter).reshape(local_len, heads_here, HEAD_DIM)
    center = jnp.mean(retained, axis=-1, keepdims=True)
    spread = jnp.mean((retained - center) ** 2, axis=-1, keepdims=True)
    normed = (retained - center) / jnp.sqrt(spread + 1e-05)
    gated = (
        (jax.nn.silu(gate_all.reshape(local_len, heads_here, HEAD_DIM)) * normed)
        .astype(jnp.bfloat16)
        .reshape(local_len, head_width)
    )
    owned = lax.all_to_all(gated, "head", split_axis=0, concat_axis=1, tiled=True)
    rows_out = lax.all_gather(w_out, "tm", axis=1, tiled=True)
    return jnp.dot(
        owned,
        lax.all_gather(rows_out, "head", axis=0, tiled=True),
        preferred_element_type=jnp.float32,
    ).astype(jnp.bfloat16)


def solution(mesh):
    return jax.shard_map(
        shards,
        mesh=mesh,
        in_specs=(
            P(("tm", "head"), None),
            P("tm", "head"),
            P("tm", "head"),
            P("tm", "head"),
            P("tm", "head"),
            P("tm", "head"),
            P("head", "tm"),
        ),
        out_specs=P(("tm", "head"), None),
        check_vma=False,
    )
```

profile of v0, /device:TPU:1, one launch (start us, length us, event | category | flops | bytes accessed | tf_op | source)
XLA Modules:
  0.0 235.8 jit_solution(7422585032205424245)
XLA Ops:
  6.5 0.0 all-gather.8.cloned.1.call-start
  6.5 0.7 all-gather.8.cloned.1.call-update
  7.3 0.0 all-gather.6.cloned.1.call-start
  7.3 1.5 pad_maximum_fusion
  8.8 0.0 all-gather.6.cloned.1.call-update
  8.8 0.0 all-gather.12.cloned.1.call-start
  8.9 1.3 reduce_sum.45
  10.2 1.0 reduce-window.6
  11.1 0.7 slice.51
  11.8 0.2 slice_reduce_fusion.1
  12.0 0.2 reduce-window.9
  12.2 0.1 broadcast.153
  12.2 0.6 slice.52
  14.2 0.1 subtract_exponential_fusion
  14.3 0.0 copy-start
  14.3 48.5 %all-gather.8.cloned.1.call-done = bf16[512,2048]{1,0:T(8,128)(2,1)} async-done(((bf16[32,2048]{1,0:T(8,128)(2,1)}), bf16[512,2048]{1,0:T(8,128)(2,1)}) %all-gather.8.cloned.1.call-update) | async-done | bytes 2097168 | tf_op jit(solution)/shard_map/all_gather | solution.py:33
  62.7 42.3 %all-gather.6.cloned.1.call-done = bf16[2048,512]{1,0:T(8,128)(2,1)} async-done(((bf16[128,512]{1,0:T(8,128)(2,1)}), bf16[2048,512]{1,0:T(8,128)(2,1)}) %all-gather.6.cloned.1.call-update) | async-done | bytes 2097168 | tf_op jit(solution)/shard_map/all_gather | solution.py:29
  105.0 3.5 %fusion.35 = (bf16[512,512]{1,0:T(8,128)(2,1)S(1)}, f32[512,512]{1,0:T(8,128)S(1)}) fusion(bf16[512,2048]{1,0:T(8,128)(2,1)} %all-gather.8.cloned.1.call-done, bf16[2048,512]{1,0:T(8,128)(2,1)} %all-gather.6.cloned.1.call-done), kind=kOutput, calls=%fused_computation.55 | convolution fusion | flops 1074003968 | bytes 5767168 | tf_op jit(solution)/shard_map/dot_general | solution.py:32
  108.5 0.3 fusion.4
  108.8 1.3 concatenate.7
  110.1 0.0 all-gather.12.cloned.1.call-update
  110.1 0.0 all-gather.10.cloned.1.call-start
  110.1 0.0 copy-done
  110.1 19.1 %all_gather.22 = bf16[128,2048]{1,0:T(8,128)(2,1)} all-gather(bf16[128,128]{1,0:T(8,128)(2,1)S(1)} %copy-done), channel_id=1, replica_groups=mesh['tm'=16,'head'=16] {'tm'}, dimensions={1}, use_global_device_ids=true | all-gather | bytes 557056 | tf_op jit(solution)/shard_map/all_gather | solution.py:96
  129.2 0.0 all-gather.10.cloned.1.call-update
  129.2 0.6 slice.49
  129.9 0.6 slice.50
  131.9 0.5 fusion.2
  132.4 14.9 %all-gather.12.cloned.1.call-done = f32[16,136,128]{2,1,0:T(8,128)} async-done(((f32[1,136,128]{2,1,0:T(8,128)}), f32[16,136,128]{2,1,0:T(8,128)}) %all-gather.12.cloned.1.call-update) | async-done | bytes 1114128 | tf_op jit(solution)/shard_map/all_gather | solution.py:15
  147.3 1.0 slice_reduce_fusion
  148.4 0.1 select_reduce_fusion
  148.5 1.4 fusion.5
  149.9 0.5 fusion.36
  150.4 0.2 fusion.13
  150.7 0.2 fusion.16
  150.9 13.2 %all_to_all.19 = bf16[16,32,128]{2,1,0:T(8,128)(2,1)S(1)} all-to-all(bf16[16,32,128]{2,1,0:T(8,128)(2,1)S(1)} %bitcast.62), channel_id=1, replica_groups=mesh['tm'=16,'head'=16] {'head'}, dimensions={0} | all-to-all | bytes 262144 | tf_op jit(solution)/shard_map/all_to_all | solution.py:95
  164.0 59.6 %all-gather.10.cloned.1.call-done = bf16[2048,2048]{1,0:T(8,128)(2,1)} async-done(((bf16[128,2048]{1,0:T(8,128)(2,1)}), bf16[2048,2048]{1,0:T(8,128)(2,1)}) %all-gather.10.cloned.1.call-update) | async-done | bytes 8388624 | tf_op jit(solution)/shard_map/all_gather | solution.py:99
  223.7 5.6 %convolution_convert_fusion = bf16[32,2048]{1,0:T(8,128)(2,1)} fusion(bf16[2048,2048]{1,0:T(8,128)(2,1)} %all-gather.10.cloned.1.call-done, bf16[16,32,128]{2,1,0:T(8,128)(2,1)S(1)} %all_to_all.19), kind=kOutput, calls=%fused_computation | convolution fusion | flops 268500992 | bytes 8650752 | tf_op jit(solution)/shard_map/dot_general | solution.py:97
  (6 shorter events, 0.0 us)
Async XLA Ops:
  6.5 56.2 %all-gather.8.cloned.1.call-start = ((), (), s32[]{:S(2)}) async-start(), calls=%async_computation.2 | async-start | bytes 2228224 | tf_op jit(solution)/shard_map/all_gather | solution.py:33
  7.3 97.7 %all-gather.6.cloned.1.call-start = ((), (), s32[]{:S(2)}) async-start(), calls=%async_computation.1 | async-start | bytes 2228224 | tf_op jit(solution)/shard_map/all_gather | solution.py:29
  8.8 138.5 %all-gather.12.cloned.1.call-start = ((), (), s32[]{:S(2)}) async-start(), calls=%async_computation.4 | async-start | bytes 1183744 | tf_op jit(solution)/shard_map/all_gather | solution.py:15
  14.3 95.9 %copy-start = (bf16[128,128]{1,0:T(8,128)(2,1)S(1)}, bf16[128,128]{1,0:T(8,128)(2,1)}, u32[]{:S(2)}) copy-start(bf16[128,128]{1,0:T(8,128)(2,1)} %param.13) | copy-start | bytes 98308
  110.1 113.6 %all-gather.10.cloned.1.call-start = ((), (), s32[]{:S(2)}) async-start(), calls=%async_computation.3 | async-start | bytes 8912896 | tf_op jit(solution)/shard_map/all_gather | solution.py:99
Sparse Core Ops, SparseCore 0:
  9.8 52.9 all-gather.7
  64.6 40.3 all-gather.5
  110.2 37.0 all-gather.11
  149.6 73.9 all-gather.9
where the time goes:
time: 236 us
  waiting for transfers between devices  166 us (70%)
  blocking collectives  32.2 us (14%)
  between operations  15.9 us (7%)
  matrix products  10.4 us (4%)
  other arithmetic  5.99 us (3%)
  local copies, waits for them, and re-layouts  5.13 us (2%)
    all_gather x1, waiting for transfers between devices, shards(): lax.all_gather(rows_out, 'head', axis=0, tiled=True)  59.6 us
    all_gather x1, waiting for transfers between devices, shards(): lax.all_gather(frames, 'head', axis=0, tiled=True)  48.5 us
    all_gather x1, waiting for transfers between devices, shards(): lax.all_gather(jnp.concatenate([w_query, w_key, w_value, w_gate], axis=1)...  42.3 us
    all_gather x1, blocking collectives, shards(): rows_out = lax.all_gather(w_out, 'tm', axis=1, tiled=True)  19.1 us
    all_gather x1, waiting for transfers between devices, prior_state(): gathered = lax.all_gather(packed, axis)  14.9 us
    all_to_all x1, blocking collectives, shards(): lax.all_to_all(gated, 'head', split_axis=0, concat_axis=1, tiled=True)  13.2 us
    dot_general x1, matrix products, shards(): jnp.dot(owned, lax.all_gather(rows_out, 'head', axis=0, tiled=True), pref...  5.58 us
  transfers between devices with their start and end apart: 4, of which 4 were waited for; matrix products, arithmetic and copies ran while one was open for 5% of the time, Pallas kernels for 0%

commit v1 on v0

--- a/solution.py
+++ b/solution.py
@@ -92,7 +92,10 @@
         .astype(jnp.bfloat16)
         .reshape(local_len, head_width)
     )
-    owned = lax.all_to_all(gated, "head", split_axis=0, concat_axis=1, tiled=True)
+    owned = jnp.concatenate(
+        lax.all_to_all(jnp.stack(jnp.split(gated, lax.axis_size("head"), axis=0)), "head", 0, 0),
+        axis=1,
+    )
     rows_out = lax.all_gather(w_out, "tm", axis=1, tiled=True)
     return jnp.dot(
         owned,

time: 236 us -> 236 us (level)
  no operation moved by 1% of the time
where the time goes in v1:
time: 236 us
  waiting for transfers between devices  166 us (70%)
  blocking collectives  32.2 us (14%)
  between operations  16 us (7%)
  matrix products  10.4 us (4%)
  other arithmetic  5.99 us (3%)
  local copies, waits for them, and re-layouts  5.27 us (2%)
    all_gather x1, waiting for transfers between devices, shards(): lax.all_gather(rows_out, 'head', axis=0, tiled=True)  59.4 us
    all_gather x1, waiting for transfers between devices, shards(): lax.all_gather(frames, 'head', axis=0, tiled=True)  48.5 us
    all_gather x1, waiting for transfers between devices, shards(): lax.all_gather(jnp.concatenate([w_query, w_key, w_value, w_gate], axis=1)...  42.3 us
    all_gather x1, blocking collectives, shards(): rows_out = lax.all_gather(w_out, 'tm', axis=1, tiled=True)  19.1 us
    all_gather x1, waiting for transfers between devices, prior_state(): gathered = lax.all_gather(packed, axis)  14.9 us
    all_to_all x1, blocking collectives, shards(): lax.all_to_all(jnp.stack(jnp.split(gated, lax.axis_size('head'), axis=0))...  13.2 us
    dot_general x1, matrix products, shards(): jnp.dot(owned, lax.all_gather(rows_out, 'head', axis=0, tiled=True), pref...  5.58 us
  transfers between devices with their start and end apart: 4, of which 4 were waited for; matrix products, arithmetic and copies ran while one was open for 5% of the time, Pallas kernels for 0%

profile of v1, /device:TPU:1, one launch (start us, length us, event | category | flops | bytes accessed | tf_op | source)
XLA Modules:
  0.0 235.8 jit_solution(14249617559605364979)
XLA Ops:
  6.5 0.0 all-gather.8.cloned.1.call-start
  6.5 0.7 all-gather.8.cloned.1.call-update
  7.3 0.0 all-gather.6.cloned.1.call-start
  7.3 1.5 pad_maximum_fusion
  8.8 0.0 all-gather.6.cloned.1.call-update
  8.8 0.0 all-gather.12.cloned.1.call-start
  8.9 1.3 reduce_sum.45
  10.2 1.0 reduce-window.6
  11.1 0.7 slice.83
  11.8 0.2 slice_reduce_fusion.1
  12.0 0.2 reduce-window.9
  12.2 0.1 broadcast.153
  12.2 0.6 slice.84
  14.2 0.1 subtract_exponential_fusion
  14.3 0.0 copy-start
  14.3 48.5 %all-gather.8.cloned.1.call-done = bf16[512,2048]{1,0:T(8,128)(2,1)} async-done(((bf16[32,2048]{1,0:T(8,128)(2,1)}), bf16[512,2048]{1,0:T(8,128)(2,1)}) %all-gather.8.cloned.1.call-update) | async-done | bytes 2097168 | tf_op jit(solution)/shard_map/all_gather | solution.py:33
  62.7 42.3 %all-gather.6.cloned.1.call-done = bf16[2048,512]{1,0:T(8,128)(2,1)} async-done(((bf16[128,512]{1,0:T(8,128)(2,1)}), bf16[2048,512]{1,0:T(8,128)(2,1)}) %all-gather.6.cloned.1.call-update) | async-done | bytes 2097168 | tf_op jit(solution)/shard_map/all_gather | solution.py:29
  105.0 3.5 %fusion.35 = (bf16[512,512]{1,0:T(8,128)(2,1)S(1)}, f32[512,512]{1,0:T(8,128)S(1)}) fusion(bf16[512,2048]{1,0:T(8,128)(2,1)} %all-gather.8.cloned.1.call-done, bf16[2048,512]{1,0:T(8,128)(2,1)} %all-gather.6.cloned.1.call-done), kind=kOutput, calls=%fused_computation.87 | convolution fusion | flops 1074003968 | bytes 5767168 | tf_op jit(solution)/shard_map/dot_general | solution.py:32
  108.5 0.3 fusion.4
  108.8 1.3 concatenate.7
  110.1 0.0 all-gather.12.cloned.1.call-update
  110.1 0.0 all-gather.10.cloned.1.call-start
  110.1 0.0 copy-done
  110.1 19.1 %all_gather.22 = bf16[128,2048]{1,0:T(8,128)(2,1)} all-gather(bf16[128,128]{1,0:T(8,128)(2,1)S(1)} %copy-done), channel_id=1, replica_groups=mesh['tm'=16,'head'=16] {'tm'}, dimensions={1}, use_global_device_ids=true | all-gather | bytes 557056 | tf_op jit(solution)/shard_map/all_gather | solution.py:99
  129.2 0.0 all-gather.10.cloned.1.call-update
  129.2 0.6 slice.81
  129.9 0.6 slice.82
  131.9 0.5 fusion.2
  132.4 14.9 %all-gather.12.cloned.1.call-done = f32[16,136,128]{2,1,0:T(8,128)} async-done(((f32[1,136,128]{2,1,0:T(8,128)}), f32[16,136,128]{2,1,0:T(8,128)}) %all-gather.12.cloned.1.call-update) | async-done | bytes 1114128 | tf_op jit(solution)/shard_map/all_gather | solution.py:15
  147.3 1.0 slice_reduce_fusion
  148.4 0.1 select_reduce_fusion
  148.5 1.4 fusion.5
  149.9 0.5 fusion.36
  150.4 0.2 fusion.13
  150.7 0.2 fusion.16
  151.1 13.2 %all_to_all.5 = bf16[16,32,128]{2,1,0:T(8,128)(2,1)S(1)} all-to-all(bf16[16,32,128]{2,1,0:T(8,128)(2,1)S(1)} %constant_dynamic-update-slice_fusion), channel_id=1, replica_groups=mesh['tm'=16,'head'=16] {'head'}, dimensions={0} | all-to-all | bytes 262144 | tf_op jit(solution)/shard_map/all_to_all | solution.py:96
  164.2 59.4 %all-gather.10.cloned.1.call-done = bf16[2048,2048]{1,0:T(8,128)(2,1)} async-done(((bf16[128,2048]{1,0:T(8,128)(2,1)}), bf16[2048,2048]{1,0:T(8,128)(2,1)}) %all-gather.10.cloned.1.call-update) | async-done | bytes 8388624 | tf_op jit(solution)/shard_map/all_gather | solution.py:102
  223.7 5.6 %convolution_convert_fusion = bf16[32,2048]{1,0:T(8,128)(2,1)} fusion(bf16[2048,2048]{1,0:T(8,128)(2,1)} %all-gather.10.cloned.1.call-done, bf16[16,32,128]{2,1,0:T(8,128)(2,1)S(1)} %all_to_all.5), kind=kOutput, calls=%fused_computation | convolution fusion | flops 268500992 | bytes 8650752 | tf_op jit(solution)/shard_map/dot_general | solution.py:100
  (22 shorter events, 0.2 us)
Async XLA Ops:
  6.5 56.2 %all-gather.8.cloned.1.call-start = ((), (), s32[]{:S(2)}) async-start(), calls=%async_computation.2 | async-start | bytes 2228224 | tf_op jit(solution)/shard_map/all_gather | solution.py:33
  7.3 97.7 %all-gather.6.cloned.1.call-start = ((), (), s32[]{:S(2)}) async-start(), calls=%async_computation.1 | async-start | bytes 2228224 | tf_op jit(solution)/shard_map/all_gather | solution.py:29
  8.8 138.5 %all-gather.12.cloned.1.call-start = ((), (), s32[]{:S(2)}) async-start(), calls=%async_computation.4 | async-start | bytes 1183744 | tf_op jit(solution)/shard_map/all_gather | solution.py:15
  14.3 95.9 %copy-start = (bf16[128,128]{1,0:T(8,128)(2,1)S(1)}, bf16[128,128]{1,0:T(8,128)(2,1)}, u32[]{:S(2)}) copy-start(bf16[128,128]{1,0:T(8,128)(2,1)} %param.13) | copy-start | bytes 98308
  110.1 113.6 %all-gather.10.cloned.1.call-start = ((), (), s32[]{:S(2)}) async-start(), calls=%async_computation.3 | async-start | bytes 8912896 | tf_op jit(solution)/shard_map/all_gather | solution.py:102
Sparse Core Ops, SparseCore 0:
  9.8 52.9 all-gather.7
  64.6 40.3 all-gather.5
  110.2 37.0 all-gather.11
  149.6 73.9 all-gather.9
